TPU v7x, 512 devices: a whole 4x4x16 slice. The times are simulated.
512 devices in a mesh: seq: 128 (over x, z, core), head: 4 (over y).
Axes of the slice: x: 4, y: 4, z: 16, core: 2. Of those that a mesh axis runs over, the one named last changes fastest.
Arguments:
- hidden: bfloat16 [32768, 2560], P(('seq', 'head')), may hold values from -6 to 6
- w_values: bfloat16 [2560, 2560], P('seq', 'head'), may hold values from -0.125 to 0.125
- w_gates: bfloat16 [2560, 2560], P('seq', 'head'), may hold values from -0.125 to 0.125
- w_steps: bfloat16 [2560, 40], P('seq', 'head'), may hold values from -0.0625 to 0.0625
- w_states: bfloat16 [2560, 256], P('seq'), may hold values from -0.125 to 0.125
- conv_weight: float32 [4, 2816], replicated, may hold values from -3 to 3
- conv_bias: float32 [2816], replicated, may hold values from -3 to 3
- step_bias: float32 [40], P('head'), may hold values from -1 to 0.5
- decay_rate: float32 [40], P('head'), may hold values from 0 to 1, as said below
- skip_gain: float32 [40], P('head'), may hold values from 1 to 8
- norm_gain: float32 [2560], replicated, may hold values from 0.5 to 1.5
- lengths: int32 [64], replicated, may hold values from 256 to 768, as said below
Outputs:
- gated_out: bfloat16 [32768, 2560], P(('seq', 'head'))
- final_states: float32 [128, 40, 64, 128], P('seq', 'head')
Inputs may be any that keep to these rules, and one draw needn't show every extreme that they name: Prompts are packed in order, each holding 256 to 768 tokens; the lengths sum to 32768. `decay_rate`: positive rates.
All inputs are finite; a program needn't handle non-finite values.
Results may differ from a plain program's by a relative error of at most 0.01.
Values may be sent and summed in bfloat16 or wider, within the bound.
No kernel may reach another device: no remote copies, remote signals or barrier semaphores. Data moves between devices by JAX's collectives and lax.ppermute only.
A program may use at most 128 MiB of HBM per device.

v0:
```python
import jax
import jax.numpy as jnp
from jax import lax
from jax.sharding import PartitionSpec as P

STRETCH = 256
epsilon = 1e-05


def from_behind(block, axis, distance):
    devices = range(lax.axis_size(axis))
    route = [(i - distance, i) for i in devices if i - distance in devices]
    return lax.ppermute(block, axis, route)


def segments_at(positions, prompt_ends):
    counted = jnp.sum((prompt_ends[None, :] <= positions[:, None]).astype(jnp.int32), axis=1)
    return jnp.where(positions < 0, -1, counted)


def on_device(
    hidden,
    w_values,
    w_gates,
    w_steps,
    w_states,
    conv_weight,
    conv_bias,
    step_bias,
    decay_rate,
    skip_gain,
    norm_gain,
    lengths,
):
    groups = lax.axis_size("head")
    group_index = lax.axis_index("head")
    block_index = lax.axis_index("seq")
    local_width = w_values.shape[1]
    inner_width = local_width * groups
    local_heads = decay_rate.shape[0]
    head_width = local_width // local_heads
    state_width = w_states.shape[1] // 2
    conv_taps = conv_weight.shape[0]
    prompt_ends = jnp.cumsum(lengths)
    block_hidden = lax.all_to_all(
        jnp.broadcast_to(hidden[None], (groups,) + hidden.shape), "head", 0, 0, tiled=True
    ).reshape(groups * hidden.shape[0], hidden.shape[1])
    block_rows = block_hidden.shape[0]
    sub_rows = block_rows // groups
    step_width = w_steps.shape[1]
    merged = jnp.concatenate([w_values, w_states, w_gates, w_steps], axis=1)
    full = lax.all_gather(merged, "seq", axis=0, tiled=True)
    projected = jnp.dot(block_hidden, full, preferred_element_type=jnp.float32)
    conv_end = local_width + 2 * state_width
    pre_rows = projected[:, :conv_end].astype(jnp.bfloat16)
    gates_sum = projected[:, conv_end : conv_end + local_width]
    steps_sum = projected[:, conv_end + local_width : conv_end + local_width + step_width]
    local_taps = jnp.concatenate(
        [
            lax.dynamic_slice_in_dim(conv_weight, group_index * local_width, local_width, 1),
            conv_weight[:, inner_width:],
        ],
        axis=1,
    )
    local_bias = jnp.concatenate(
        [
            lax.dynamic_slice_in_dim(conv_bias, group_index * local_width, local_width, 0),
            conv_bias[inner_width:],
        ],
        axis=0,
    )
    block_start = block_index * block_rows
    rim_rows = pre_rows[block_rows - (conv_taps - 1) :]
    prior_rim = from_behind(rim_rows, "seq", 1)
    extended = jnp.concatenate([prior_rim, pre_rows], axis=0)
    ext_positions = (
        block_start - (conv_taps - 1) + jnp.arange(block_rows + conv_taps - 1, dtype=jnp.int32)
    )
    ext_ids = segments_at(ext_positions, prompt_ends)
    own_ids = ext_ids[conv_taps - 1 :]
    filtered = jnp.zeros(pre_rows.shape, jnp.float32) + local_bias[None, :]
    for offset in range(conv_taps):
        matches = (ext_ids[offset : offset + block_rows] == own_ids).astype(jnp.float32)
        filtered = (
            filtered
            + local_taps[offset][None, :]
            * extended[offset : offset + block_rows].astype(jnp.float32)
            * matches[:, None]
        )
    conv_out = jax.nn.silu(filtered).astype(jnp.bfloat16)
    head_values = conv_out[:, :local_width]
    both_states = conv_out[:, local_width:]
    stretch_rows = STRETCH
    stretches = block_rows // stretch_rows
    positions = block_start + jnp.arange(block_rows, dtype=jnp.int32)
    segment_ids = segments_at(positions, prompt_ends)
    next_ids = segments_at(positions + 1, prompt_ends)
    before_ids = segments_at(positions - 1, prompt_ends)
    stretch_ids = segment_ids.reshape(stretches, stretch_rows)
    prior_ids = before_ids.reshape(stretches, stretch_rows)[:, 0]
    ends_mask = (segment_ids != next_ids).reshape(stretches, stretch_rows)
    step_sizes = jax.nn.softplus(steps_sum + step_bias[None, :])
    decay_steps = step_sizes * decay_rate[None, :]
    log_decay = -jnp.cumsum(decay_steps.reshape(stretches, stretch_rows, local_heads), axis=1)
    decay_heads = jnp.swapaxes(log_decay, 1, 2)
    step_heads = jnp.swapaxes(step_sizes.reshape(stretches, stretch_rows, local_heads), 1, 2)
    values = head_values.reshape(stretches, stretch_rows, local_heads, head_width)
    write_state = both_states[:, :state_width].reshape(stretches, stretch_rows, state_width)
    read_state = both_states[:, state_width:].reshape(stretches, stretch_rows, state_width)
    intersection = jnp.einsum(
        "ctn,csn->cts", read_state, write_state, preferred_element_type=jnp.float32
    )
    token_order = jnp.arange(stretch_rows, dtype=jnp.int32)
    causal = token_order[:, None] >= token_order[None, :]
    allowed = causal[None] & (stretch_ids[:, :, None] == stretch_ids[:, None, :])
    spread = decay_heads[:, :, :, None] - decay_heads[:, :, None, :]
    weights = (
        jnp.where(allowed[:, None], jnp.exp(jnp.minimum(spread, 0.0)), 0.0)
        * step_heads[:, :, None, :]
    )
    scores = (intersection[:, None] * weights).astype(jnp.bfloat16)
    within_stretch = jnp.einsum(
        "chts,cshp->cthp", scores, values, preferred_element_type=jnp.float32
    )
    last_ids = stretch_ids[:, -1]
    tail_decay = decay_heads[:, :, -1:]
    keep_tail = (stretch_ids == last_ids[:, None])[:, None, :]
    tail_coef = (
        jnp.where(keep_tail, jnp.exp(jnp.minimum(tail_decay - decay_heads, 0.0)), 0.0) * step_heads
    )
    tail_rows = (values.astype(jnp.float32) * jnp.swapaxes(tail_coef, 1, 2)[:, :, :, None]).astype(
        jnp.bfloat16
    )
    stretch_states = jnp.einsum(
        "clhp,cln->chpn", tail_rows, write_state, preferred_element_type=jnp.float32
    )
    stretch_gates = (
        jnp.exp(decay_heads[:, :, -1]) * (last_ids == prior_ids).astype(jnp.float32)[:, None]
    )
    own_pair = (stretch_gates[0], stretch_states[0])
    g1, s1 = from_behind(own_pair, "seq", 1)
    g2, s2 = from_behind(own_pair, "seq", 2)
    g3, s3 = from_behind(own_pair, "seq", 3)
    incoming = s1 + g1[:, None, None] * (s2 + g2[:, None, None] * s3)
    arriving = incoming[None]
    carry_mask = (stretch_ids == prior_ids[:, None]).astype(jnp.float32)
    carry_decay = jnp.exp(log_decay) * carry_mask[:, :, None]
    from_before = (
        jnp.einsum(
            "cln,chpn->clhp",
            read_state,
            arriving.astype(jnp.bfloat16),
            preferred_element_type=jnp.float32,
        )
        * carry_decay[:, :, :, None]
    )
    result = (
        within_stretch + from_before + skip_gain[None, None, :, None] * values.astype(jnp.float32)
    )
    ssm_rows = result.reshape(block_rows, local_width).astype(jnp.bfloat16)
    end_weight = ends_mask.astype(jnp.float32)
    has_end = jnp.sum(end_weight, axis=1)
    end_decay = jnp.sum(decay_heads * end_weight[:, None, :], axis=2)
    end_ids = jnp.sum(jnp.where(ends_mask, stretch_ids, 0), axis=1)
    keep_end = ((stretch_ids == end_ids[:, None]) & (has_end[:, None] > 0))[:, None, :]
    end_coef = (
        jnp.where(keep_end, jnp.exp(jnp.minimum(end_decay[:, :, None] - decay_heads, 0.0)), 0.0)
        * step_heads
    )
    end_rows = (values.astype(jnp.float32) * jnp.swapaxes(end_coef, 1, 2)[:, :, :, None]).astype(
        jnp.bfloat16
    )
    end_states = jnp.einsum(
        "clhp,cln->chpn", end_rows, write_state, preferred_element_type=jnp.float32
    )
    end_carry = (
        jnp.exp(end_decay) * ((end_ids == prior_ids) & (has_end > 0)).astype(jnp.float32)[:, None]
    )
    end_states = end_states + end_carry[:, :, None, None] * arriving
    final_block = jnp.sum(end_states, axis=0)[None]
    head_gates = gates_sum.astype(jnp.bfloat16)
    both = jnp.stack([ssm_rows, head_gates]).reshape(2, groups, sub_rows, local_width)
    returned = lax.all_to_all(both, "head", split_axis=1, concat_axis=3, tiled=True)
    token_rows = returned.reshape(2, sub_rows, inner_width).astype(jnp.float32)
    gated = token_rows[0] * jax.nn.silu(token_rows[1])
    mean_square = jnp.mean(gated * gated, axis=1)
    scaled = gated * lax.rsqrt(mean_square + epsilon)[:, None] * norm_gain[None, :]
    gated_out = scaled.astype(jnp.bfloat16)
    return (gated_out, final_block)


def solution(mesh):
    in_specs = (
        P(("seq", "head"), None),
        P("seq", "head"),
        P("seq", "head"),
        P("seq", "head"),
        P("seq", None),
        P(),
        P(),
        P("head"),
        P("head"),
        P("head"),
        P(),
        P(),
    )
    out_specs = (P(("seq", "head"), None), P("seq", "head", None, None))
    return jax.shard_map(
        on_device, mesh=mesh, in_specs=in_specs, out_specs=out_specs, check_vma=False
    )
```

profile of v0, /device:TPU:5, one launch (start us, length us, event | category | flops | bytes accessed | tf_op | source)
XLA Modules:
  0.0 259.8 jit_solution(16076834221550302030)
XLA Ops:
  7.2 0.8 copy.65
  8.0 1.4 maximum_bitcast_fusion
  9.5 2.1 broadcast_in_dim.39
  11.6 4.3 %all-to-all-start = ((bf16[4,64,2560]{2,1,0:T(8,128)(2,1)}), bf16[4,64,2560]{2,1,0:T(8,128)(2,1)S(1)}, u32[]{:S(2)}, u32[]{:S(2)}) async-start(bf16[4,64,2560]{2,1,0:T(8,128)(2,1)} %broadcast_in_dim.39), calls=%async_computation | async-start | bytes 2621440 | tf_op jit(solution)/shard_map/all_to_all | solution.py:45
  16.2 0.7 slice.91
  16.9 0.8 dynamic_slice.6
  24.3 0.7 broadcast_compare_fusion
  25.1 139.3 %all-gather.3.cloned.1.call-done = bf16[128,20,1546]{2,1,0:T(8,128)(2,1)} async-done(((bf16[1,20,1546]{2,1,0:T(8,128)(2,1)}), bf16[128,20,1546]{2,1,0:T(8,128)(2,1)}) %all-gather.3.cloned.1.call-update) | async-done | bytes 7915536 | tf_op jit(solution)/shard_map/all_gather | solution.py:52
  164.5 13.7 %reshape.504 = bf16[2560,1546]{1,0:T(8,128)(2,1)} reshape(bf16[128,20,1546]{2,1,0:T(8,128)(2,1)} %all-gather.3.cloned.1.call-done) | data formatting | bytes 15831040
  178.2 5.8 %fusion.50 = (bf16[256,1546]{0,1:T(8,128)(2,1)S(1)}, f32[256,1546]{0,1:T(8,128)S(1)}) fusion(bf16[2560,1546]{1,0:T(8,128)(2,1)} %reshape.504, bf16[256,2560]{1,0:T(8,128)(2,1)S(1)} %bitcast.126), kind=kOutput, calls=%fused_computation.113 | convolution fusion | flops 2026768896 | bytes 11600896 | tf_op jit(solution)/shard_map/dot_general | solution.py:53
  184.2 1.0 copy-done.4
  186.4 0.8 fusion.31
  187.4 3.4 %collective-permute-start.4 = (f32[10]{0:T(128)S(1)}, f32[10]{0:T(128)S(1)}, u32[]{:S(2)}, u32[]{:S(2)}) collective-permute-start(f32[10]{0:T(128)S(1)} %exponential_multiply_fusion.1), channel_id=1, source_target_pairs={{0,8},{4,12},{8,16},{12,20},{16,24},{20,28},{24,32},{28,36},{32,40... | collective-permute-start | bytes 128 | tf_op jit(solution)/shard_map/ppermute | solution.py:13
  190.8 2.8 %collective-permute-start.2 = (f32[10]{0:T(128)S(1)}, f32[10]{0:T(128)S(1)}, u32[]{:S(2)}, u32[]{:S(2)}) collective-permute-start(f32[10]{0:T(128)S(1)} %exponential_multiply_fusion.1), channel_id=1, source_target_pairs={{0,4},{4,8},{8,12},{12,16},{16,20},{20,24},{24,28},{28,32},{32,36}... | collective-permute-start | bytes 128 | tf_op jit(solution)/shard_map/ppermute | solution.py:13
  193.8 1.9 collective-permute-start
  195.8 0.8 fusion.32
  196.9 0.8 copy.75
  197.7 0.9 collective-permute-done
  198.7 1.5 multiply_convert_fusion.4
  200.2 0.8 fusion.12
  201.3 4.4 %collective-permute-start.1 = (f32[10,64,128]{2,1,0:T(8,128)S(1)}, f32[10,64,128]{2,1,0:T(8,128)S(1)}, u32[]{:S(2)}, u32[]{:S(2)}) collective-permute-start(f32[10,64,128]{2,1,0:T(8,128)S(1)} %fusion.20), channel_id=1, source_target_pairs={{0,4},{4,8},{8,12},{12,16},{16,20},{20,24},{24,28},{28,32},{32,36}... | collective-permute-start | bytes 983048 | tf_op jit(solution)/shard_map/ppermute | solution.py:13
  205.7 3.0 %collective-permute-start.3 = (f32[10,64,128]{2,1,0:T(8,128)S(1)}, f32[10,64,128]{2,1,0:T(8,128)S(1)}, u32[]{:S(2)}, u32[]{:S(2)}) collective-permute-start(f32[10,64,128]{2,1,0:T(8,128)S(1)} %fusion.20), channel_id=1, source_target_pairs={{0,8},{4,12},{8,16},{12,20},{16,24},{20,28},{24,32},{28,36},{32,40... | collective-permute-start | bytes 983048 | tf_op jit(solution)/shard_map/ppermute | solution.py:13
  208.7 2.5 collective-permute-start.5
  211.4 0.9 fusion.7
  212.4 11.8 %collective-permute-done.3 = f32[10,64,128]{2,1,0:T(8,128)S(1)} collective-permute-done((f32[10,64,128]{2,1,0:T(8,128)S(1)}, f32[10,64,128]{2,1,0:T(8,128)S(1)}, u32[]{:S(2)}, u32[]{:S(2)}) %collective-permute-start.3) | collective-permute-done | bytes 327712 | tf_op jit(solution)/shard_map/ppermute | solution.py:13
  224.2 7.7 %collective-permute-done.5 = f32[10,64,128]{2,1,0:T(8,128)S(1)} collective-permute-done((f32[10,64,128]{2,1,0:T(8,128)S(1)}, f32[10,64,128]{2,1,0:T(8,128)S(1)}, u32[]{:S(2)}, u32[]{:S(2)}) %collective-permute-start.5) | collective-permute-done | bytes 327712 | tf_op jit(solution)/shard_map/ppermute | solution.py:13
  232.6 1.1 pad_maximum_fusion
  233.7 2.4 copy.76
  236.1 4.0 %all-to-all-start.1 = ((bf16[2,4,64,640]{3,2,0,1:T(8,128)(2,1)}), bf16[2,4,64,640]{3,2,0,1:T(8,128)(2,1)S(1)}, u32[]{:S(2)}, u32[]{:S(2)}) async-start(bf16[2,4,64,640]{3,2,0,1:T(8,128)(2,1)} %copy.76), calls=%async_computation.1 | async-start | bytes 1310720 | tf_op jit(solution)/shard_map/all_to_all | solution.py:183
  240.8 1.0 add_bitcast_fusion
  241.8 8.4 %all-to-all-done.1 = bf16[2,4,64,640]{3,2,0,1:T(8,128)(2,1)S(1)} async-done(((bf16[2,4,64,640]{3,2,0,1:T(8,128)(2,1)}), bf16[2,4,64,640]{3,2,0,1:T(8,128)(2,1)S(1)}, u32[]{:S(2)}, u32[]{:S(2)}) %all-to-all-start.1) | async-done | bytes 655392 | tf_op jit(solution)/shard_map/all_to_all | solution.py:183
  252.1 0.8 multiply_convert_fusion.5
  (84 shorter events, 8.7 us)
Async XLA Ops:
  7.2 157.3 %all-gather.3.cloned.1.call-start = ((), (), s32[]{:S(2)}) async-start(), calls=%async_computation.2 | async-start | bytes 10303488 | tf_op jit(solution)/shard_map/all_gather | solution.py:52
  11.6 4.3 %copy-start.5 = (s32[64]{0:T(128)S(1)}, s32[64]{0:T(128)}, u32[]{:S(2)}) copy-start(s32[64]{0:T(128)} %param.23) | copy-start | bytes 772
  11.6 11.8 %copy-start.1 = (f32[4,2816]{1,0:T(4,128)S(1)}, f32[4,2816]{1,0:T(4,128)}, u32[]{:S(2)}) copy-start(f32[4,2816]{1,0:T(4,128)} %param.17) | copy-start | bytes 135172
  11.6 11.8 %slice-start = ((f32[4,2816]{1,0:T(4,128)}), f32[4,256]{1,0:T(4,128)S(1)}, s32[]{:S(2)}) async-start(f32[4,2816]{1,0:T(4,128)} %param.17), calls=%async_computation.3 | async-start | bytes 8192 | tf_op jit(solution)/shard_map/slice | solution.py:61
  11.6 166.6 %all-to-all-start = ((bf16[4,64,2560]{2,1,0:T(8,128)(2,1)}), bf16[4,64,2560]{2,1,0:T(8,128)(2,1)S(1)}, u32[]{:S(2)}, u32[]{:S(2)}) async-start(bf16[4,64,2560]{2,1,0:T(8,128)(2,1)} %broadcast_in_dim.39), calls=%async_computation | async-start | bytes 2621440 | tf_op jit(solution)/shard_map/all_to_all | solution.py:45
  178.2 5.9 %copy-start.3 = (f32[10]{0:T(128)S(1)}, f32[10]{0:T(128)}, u32[]{:S(2)}) copy-start(f32[10]{0:T(128)} %param.19) | copy-start | bytes 124
  178.2 5.9 %copy-start.6 = (f32[10]{0:T(128)S(1)}, f32[10]{0:T(128)}, u32[]{:S(2)}) copy-start(f32[10]{0:T(128)} %param.20) | copy-start | bytes 124
  184.0 1.2 copy-start.4
  187.4 24.9 %collective-permute-start.4 = (f32[10]{0:T(128)S(1)}, f32[10]{0:T(128)S(1)}, u32[]{:S(2)}, u32[]{:S(2)}) collective-permute-start(f32[10]{0:T(128)S(1)} %exponential_multiply_fusion.1), channel_id=1, source_target_pairs={{0,8},{4,12},{8,16},{12,20},{16,24},{20,28},{24,32},{28,36},{32,40... | collective-permute-start | bytes 128 | tf_op jit(solution)/shard_map/ppermute | solution.py:13
  190.8 21.5 %collective-permute-start.2 = (f32[10]{0:T(128)S(1)}, f32[10]{0:T(128)S(1)}, u32[]{:S(2)}, u32[]{:S(2)}) collective-permute-start(f32[10]{0:T(128)S(1)} %exponential_multiply_fusion.1), channel_id=1, source_target_pairs={{0,4},{4,8},{8,12},{12,16},{16,20},{20,24},{24,28},{28,32},{32,36}... | collective-permute-start | bytes 128 | tf_op jit(solution)/shard_map/ppermute | solution.py:13
  193.8 4.9 %collective-permute-start = (bf16[3,896]{0,1:T(8,128)(2,1)S(1)}, bf16[3,896]{0,1:T(8,128)(2,1)S(1)}, u32[]{:S(2)}, u32[]{:S(2)}) collective-permute-start(bf16[3,896]{0,1:T(8,128)(2,1)S(1)} %slice.120), channel_id=1, source_target_pairs={{0,4},{4,8},{8,12},{12,16},{16,20},{20,24},{24,28},{28,32},{32,36}... | collective-permute-start | bytes 16136 | tf_op jit(solution)/shard_map/ppermute | solution.py:13
  201.3 11.0 %collective-permute-start.1 = (f32[10,64,128]{2,1,0:T(8,128)S(1)}, f32[10,64,128]{2,1,0:T(8,128)S(1)}, u32[]{:S(2)}, u32[]{:S(2)}) collective-permute-start(f32[10,64,128]{2,1,0:T(8,128)S(1)} %fusion.20), channel_id=1, source_target_pairs={{0,4},{4,8},{8,12},{12,16},{16,20},{20,24},{24,28},{28,32},{32,36}... | collective-permute-start | bytes 983048 | tf_op jit(solution)/shard_map/ppermute | solution.py:13
  205.7 18.5 %collective-permute-start.3 = (f32[10,64,128]{2,1,0:T(8,128)S(1)}, f32[10,64,128]{2,1,0:T(8,128)S(1)}, u32[]{:S(2)}, u32[]{:S(2)}) collective-permute-start(f32[10,64,128]{2,1,0:T(8,128)S(1)} %fusion.20), channel_id=1, source_target_pairs={{0,8},{4,12},{8,16},{12,20},{16,24},{20,28},{24,32},{28,36},{32,40... | collective-permute-start | bytes 983048 | tf_op jit(solution)/shard_map/ppermute | solution.py:13
  208.7 23.2 %collective-permute-start.5 = (f32[10,64,128]{2,1,0:T(8,128)S(1)}, f32[10,64,128]{2,1,0:T(8,128)S(1)}, u32[]{:S(2)}, u32[]{:S(2)}) collective-permute-start(f32[10,64,128]{2,1,0:T(8,128)S(1)} %fusion.20), channel_id=1, source_target_pairs={{0,12},{4,16},{8,20},{12,24},{16,28},{20,32},{24,36},{28,40},{32,4... | collective-permute-start | bytes 983048 | tf_op jit(solution)/shard_map/ppermute | solution.py:13
  211.4 20.7 %copy-start.7 = (f32[10]{0:T(128)S(1)}, f32[10]{0:T(128)}, u32[]{:S(2)}) copy-start(f32[10]{0:T(128)} %param.21) | copy-start | bytes 124
  233.7 7.1 %copy-start = (bf16[256,640]{0,1:T(8,128)(2,1)S(1)}, bf16[256,640]{0,1:T(8,128)(2,1)}, u32[]{:S(2)}) copy-start(bf16[256,640]{0,1:T(8,128)(2,1)} %get-tuple-element.20) | copy-start | bytes 983044
  236.1 14.1 %all-to-all-start.1 = ((bf16[2,4,64,640]{3,2,0,1:T(8,128)(2,1)}), bf16[2,4,64,640]{3,2,0,1:T(8,128)(2,1)S(1)}, u32[]{:S(2)}, u32[]{:S(2)}) async-start(bf16[2,4,64,640]{3,2,0,1:T(8,128)(2,1)} %copy.76), calls=%async_computation.1 | async-start | bytes 1310720 | tf_op jit(solution)/shard_map/all_to_all | solution.py:183
  251.4 0.7 copy-start.2
Sparse Core Ops, SparseCore 0:
  11.7 152.7 all-gather.2
where the time goes:
time: 261 us; the launch traced here: 260 us
  waiting for transfers between devices  168 us (64%)
  local copies, waits for them, and re-layouts  26.9 us (10%)
  starting transfers between devices  26.3 us (10%)
  between operations  18.4 us (7%)
  other arithmetic  11.4 us (4%)
  matrix products  8.44 us (3%)
    all_gather x1, waiting for transfers between devices, on_device(): full = lax.all_gather(merged, 'seq', axis=0, tiled=True)  139 us
    ppermute x6, waiting for transfers between devices, from_behind(): return lax.ppermute(block, axis, route)  20.5 us
    ppermute x6, starting transfers between devices, from_behind(): return lax.ppermute(block, axis, route)  18 us
    unnamed x24, local copies, waits for them, and re-layouts  16 us
    all_to_all x1, waiting for transfers between devices, on_device(): lax.all_to_all(both, 'head', split_axis=1, concat_axis=3, tiled=True)  8.45 us
    dot_general x1, matrix products, on_device(): projected = jnp.dot(block_hidden, full, preferred_element_type=jnp.float32)  5.84 us
  transfers between devices with their start and end apart: 9, of which 5 were waited for; matrix products, arithmetic and copies ran while one was open for 11% of the time, Pallas kernels for 0%

commit v1 on v0

--- a/solution.py
+++ b/solution.py
@@ -180,7 +180,10 @@
     final_block = jnp.sum(end_states, axis=0)[None]
     head_gates = gates_sum.astype(jnp.bfloat16)
     both = jnp.stack([ssm_rows, head_gates]).reshape(2, groups, sub_rows, local_width)
-    returned = lax.all_to_all(both, "head", split_axis=1, concat_axis=3, tiled=True)
+    returned = jnp.concatenate(
+        lax.all_to_all(jnp.stack(jnp.split(both, lax.axis_size("head"), axis=1)), "head", 0, 0),
+        axis=3,
+    )
     token_rows = returned.reshape(2, sub_rows, inner_width).astype(jnp.float32)
     gated = token_rows[0] * jax.nn.silu(token_rows[1])
     mean_square = jnp.mean(gated * gated, axis=1)

time: 261 us -> 268 us (1.027)
  other arithmetic: 11.4 us -> 17.7 us
    another operation x1, other arithmetic: 1.1 us -> 6.54 us  [on_device(): jnp.stack([ssm_rows, head_gates]).reshape(2, groups, sub_rows, local_width)]
    unnamed x24 -> x26, local copies, waits for them, and re-layouts: 16 us -> 16 us
where the time goes in v1:
time: 268 us; the launch traced here: 267 us
  waiting for transfers between devices  168 us (63%)
  local copies, waits for them, and re-layouts  27.9 us (10%)
  starting transfers between devices  26.3 us (10%)
  between operations  18.3 us (7%)
  other arithmetic  17.7 us (7%)
  matrix products  8.43 us (3%)
    all_gather x1, waiting for transfers between devices, on_device(): full = lax.all_gather(merged, 'seq', axis=0, tiled=True)  139 us
    ppermute x6, waiting for transfers between devices, from_behind(): return lax.ppermute(block, axis, route)  20.1 us
    ppermute x6, starting transfers between devices, from_behind(): return lax.ppermute(block, axis, route)  18 us
    unnamed x26, local copies, waits for them, and re-layouts  16 us
    all_to_all x1, waiting for transfers between devices, on_device(): lax.all_to_all(jnp.stack(jnp.split(both, lax.axis_size('head'), axis=1)),...  8.55 us
    another operation x1, other arithmetic, on_device(): jnp.stack([ssm_rows, head_gates]).reshape(2, groups, sub_rows, local_width)  6.54 us
    dot_general x1, matrix products, on_device(): projected = jnp.dot(block_hidden, full, preferred_element_type=jnp.float32)  5.84 us
  transfers between devices with their start and end apart: 9, of which 5 were waited for; matrix products, arithmetic and copies ran while one was open for 11% of the time, Pallas kernels for 0%

profile of v1, /device:TPU:5, one launch (start us, length us, event | category | flops | bytes accessed | tf_op | source)
XLA Modules:
  0.0 266.8 jit_solution(9039778688504044191)
XLA Ops:
  7.2 0.8 copy.139
  8.0 1.4 maximum_bitcast_fusion
  9.5 2.1 broadcast_in_dim.39
  11.6 4.3 %all-to-all-start = ((bf16[4,64,2560]{2,1,0:T(8,128)(2,1)}), bf16[4,64,2560]{2,1,0:T(8,128)(2,1)S(1)}, u32[]{:S(2)}, u32[]{:S(2)}) async-start(bf16[4,64,2560]{2,1,0:T(8,128)(2,1)} %broadcast_in_dim.39), calls=%async_computation | async-start | bytes 2621440 | tf_op jit(solution)/shard_map/all_to_all | solution.py:45
  16.2 0.7 slice.91
  16.9 0.8 dynamic_slice.6
  25.0 139.4 %all-gather.3.cloned.1.call-done = bf16[128,20,1546]{2,1,0:T(8,128)(2,1)} async-done(((bf16[1,20,1546]{2,1,0:T(8,128)(2,1)}), bf16[128,20,1546]{2,1,0:T(8,128)(2,1)}) %all-gather.3.cloned.1.call-update) | async-done | bytes 7915536 | tf_op jit(solution)/shard_map/all_gather | solution.py:52
  164.5 13.7 %reshape.500 = bf16[2560,1546]{1,0:T(8,128)(2,1)} reshape(bf16[128,20,1546]{2,1,0:T(8,128)(2,1)} %all-gather.3.cloned.1.call-done) | data formatting | bytes 15831040
  178.2 5.8 %fusion.53 = (bf16[256,1546]{0,1:T(8,128)(2,1)S(1)}, f32[256,1546]{0,1:T(8,128)S(1)}) fusion(bf16[2560,1546]{1,0:T(8,128)(2,1)} %reshape.500, bf16[256,2560]{1,0:T(8,128)(2,1)S(1)} %bitcast.127), kind=kOutput, calls=%fused_computation.123 | convolution fusion | flops 2026768896 | bytes 11600896 | tf_op jit(solution)/shard_map/dot_general | solution.py:53
  184.2 1.0 copy-done.5
  186.4 0.8 fusion.34
  187.4 3.4 %collective-permute-start.4 = (f32[10]{0:T(128)S(1)}, f32[10]{0:T(128)S(1)}, u32[]{:S(2)}, u32[]{:S(2)}) collective-permute-start(f32[10]{0:T(128)S(1)} %exponential_multiply_fusion.1), channel_id=1, source_target_pairs={{0,8},{4,12},{8,16},{12,20},{16,24},{20,28},{24,32},{28,36},{32,40... | collective-permute-start | bytes 128 | tf_op jit(solution)/shard_map/ppermute | solution.py:13
  190.8 2.8 %collective-permute-start.2 = (f32[10]{0:T(128)S(1)}, f32[10]{0:T(128)S(1)}, u32[]{:S(2)}, u32[]{:S(2)}) collective-permute-start(f32[10]{0:T(128)S(1)} %exponential_multiply_fusion.1), channel_id=1, source_target_pairs={{0,4},{4,8},{8,12},{12,16},{16,20},{20,24},{24,28},{28,32},{32,36}... | collective-permute-start | bytes 128 | tf_op jit(solution)/shard_map/ppermute | solution.py:13
  193.8 1.9 collective-permute-start
  195.8 0.8 fusion.35
  196.9 1.3 copy.149
  198.7 1.5 multiply_convert_fusion.4
  200.2 0.8 fusion.15
  201.3 4.4 %collective-permute-start.1 = (f32[10,64,128]{2,1,0:T(8,128)S(1)}, f32[10,64,128]{2,1,0:T(8,128)S(1)}, u32[]{:S(2)}, u32[]{:S(2)}) collective-permute-start(f32[10,64,128]{2,1,0:T(8,128)S(1)} %fusion.23), channel_id=1, source_target_pairs={{0,4},{4,8},{8,12},{12,16},{16,20},{20,24},{24,28},{28,32},{32,36}... | collective-permute-start | bytes 983048 | tf_op jit(solution)/shard_map/ppermute | solution.py:13
  205.7 3.0 %collective-permute-start.3 = (f32[10,64,128]{2,1,0:T(8,128)S(1)}, f32[10,64,128]{2,1,0:T(8,128)S(1)}, u32[]{:S(2)}, u32[]{:S(2)}) collective-permute-start(f32[10,64,128]{2,1,0:T(8,128)S(1)} %fusion.23), channel_id=1, source_target_pairs={{0,8},{4,12},{8,16},{12,20},{16,24},{20,28},{24,32},{28,36},{32,40... | collective-permute-start | bytes 983048 | tf_op jit(solution)/shard_map/ppermute | solution.py:13
  208.7 2.5 collective-permute-start.5
  211.4 0.9 fusion.7
  212.4 11.8 %collective-permute-done.3 = f32[10,64,128]{2,1,0:T(8,128)S(1)} collective-permute-done((f32[10,64,128]{2,1,0:T(8,128)S(1)}, f32[10,64,128]{2,1,0:T(8,128)S(1)}, u32[]{:S(2)}, u32[]{:S(2)}) %collective-permute-start.3) | collective-permute-done | bytes 327712 | tf_op jit(solution)/shard_map/ppermute | solution.py:13
  224.2 7.7 %collective-permute-done.5 = f32[10,64,128]{2,1,0:T(8,128)S(1)} collective-permute-done((f32[10,64,128]{2,1,0:T(8,128)S(1)}, f32[10,64,128]{2,1,0:T(8,128)S(1)}, u32[]{:S(2)}, u32[]{:S(2)}) %collective-permute-start.5) | collective-permute-done | bytes 327712 | tf_op jit(solution)/shard_map/ppermute | solution.py:13
  232.3 1.1 convert_element_type.162
  233.5 6.5 %fusion.13 = (bf16[2,1,64,640]{2,1,3,0:T(2,128)(2,1)S(1)}, bf16[2,1,64,640]{2,1,3,0:T(2,128)(2,1)S(1)}, bf16[2,1,64,640]{2,1,3,0:T(2,128)(2,1)S(1)}, bf16[2,1,64,640]{2,1,3,0:T(2,128)(2,1)S(1)}) fusion(bf16[1,4,64,640]{2,1,3,0:T(4,128)(2,1)} %convert_element_type.162, bf16[1,4,64,640]{2,1,3,0:T(4,128)(2,1)} %copy.149), kind=kLoop, calls=%fused_computation.28 | loop fusion | flops 1310720 | bytes 1310720 | tf_op jit(solution)/shard_map/stack | solution.py:182
  240.0 1.0 copy.153
  242.2 0.9 pad_maximum_fusion.1
  243.2 4.0 %all-to-all-start.1 = ((bf16[4,2,1,64,640]{4,3,1,2,0:T(8,128)(2,1)}), bf16[4,2,1,64,640]{4,3,1,2,0:T(8,128)(2,1)S(1)}, u32[]{:S(2)}, u32[]{:S(2)}) async-start(bf16[4,2,1,64,640]{4,3,1,2,0:T(8,128)(2,1)} %pad_maximum_fusion.1), calls=%async_computation.1 | async-start | bytes 1310720 | tf_op jit(solution)/shard_map/all_to_all | solution.py:184
  247.8 1.0 add_bitcast_fusion
  248.8 8.6 %all-to-all-done.1 = bf16[4,2,1,64,640]{4,3,1,2,0:T(8,128)(2,1)S(1)} async-done(((bf16[4,2,1,64,640]{4,3,1,2,0:T(8,128)(2,1)}), bf16[4,2,1,64,640]{4,3,1,2,0:T(8,128)(2,1)S(1)}, u32[]{:S(2)}, u32[]{:S(2)}) %all-to-all-start.1) | async-done | bytes 655392 | tf_op jit(solution)/shard_map/all_to_all | solution.py:184
  259.1 0.8 multiply_convert_fusion.5
  (90 shorter events, 10.6 us)
Async XLA Ops:
  7.2 157.3 %all-gather.3.cloned.1.call-start = ((), (), s32[]{:S(2)}) async-start(), calls=%async_computation.2 | async-start | bytes 10303488 | tf_op jit(solution)/shard_map/all_gather | solution.py:52
  11.6 4.3 %copy-start.6 = (s32[64]{0:T(128)S(1)}, s32[64]{0:T(128)}, u32[]{:S(2)}) copy-start(s32[64]{0:T(128)} %param.23) | copy-start | bytes 772
  11.6 11.8 %copy-start.2 = (f32[4,2816]{1,0:T(4,128)S(1)}, f32[4,2816]{1,0:T(4,128)}, u32[]{:S(2)}) copy-start(f32[4,2816]{1,0:T(4,128)} %param.17) | copy-start | bytes 135172
  11.6 11.8 %slice-start = ((f32[4,2816]{1,0:T(4,128)}), f32[4,256]{1,0:T(4,128)S(1)}, s32[]{:S(2)}) async-start(f32[4,2816]{1,0:T(4,128)} %param.17), calls=%async_computation.3 | async-start | bytes 8192 | tf_op jit(solution)/shard_map/slice | solution.py:61
  11.6 166.6 %all-to-all-start = ((bf16[4,64,2560]{2,1,0:T(8,128)(2,1)}), bf16[4,64,2560]{2,1,0:T(8,128)(2,1)S(1)}, u32[]{:S(2)}, u32[]{:S(2)}) async-start(bf16[4,64,2560]{2,1,0:T(8,128)(2,1)} %broadcast_in_dim.39), calls=%async_computation | async-start | bytes 2621440 | tf_op jit(solution)/shard_map/all_to_all | solution.py:45
  178.2 5.9 %copy-start.4 = (f32[10]{0:T(128)S(1)}, f32[10]{0:T(128)}, u32[]{:S(2)}) copy-start(f32[10]{0:T(128)} %param.19) | copy-start | bytes 124
  178.2 5.9 %copy-start.7 = (f32[10]{0:T(128)S(1)}, f32[10]{0:T(128)}, u32[]{:S(2)}) copy-start(f32[10]{0:T(128)} %param.20) | copy-start | bytes 124
  184.0 1.2 copy-start.5
  187.4 24.9 %collective-permute-start.4 = (f32[10]{0:T(128)S(1)}, f32[10]{0:T(128)S(1)}, u32[]{:S(2)}, u32[]{:S(2)}) collective-permute-start(f32[10]{0:T(128)S(1)} %exponential_multiply_fusion.1), channel_id=1, source_target_pairs={{0,8},{4,12},{8,16},{12,20},{16,24},{20,28},{24,32},{28,36},{32,40... | collective-permute-start | bytes 128 | tf_op jit(solution)/shard_map/ppermute | solution.py:13
  190.8 21.5 %collective-permute-start.2 = (f32[10]{0:T(128)S(1)}, f32[10]{0:T(128)S(1)}, u32[]{:S(2)}, u32[]{:S(2)}) collective-permute-start(f32[10]{0:T(128)S(1)} %exponential_multiply_fusion.1), channel_id=1, source_target_pairs={{0,4},{4,8},{8,12},{12,16},{16,20},{20,24},{24,28},{28,32},{32,36}... | collective-permute-start | bytes 128 | tf_op jit(solution)/shard_map/ppermute | solution.py:13
  193.8 4.9 %collective-permute-start = (bf16[3,896]{0,1:T(8,128)(2,1)S(1)}, bf16[3,896]{0,1:T(8,128)(2,1)S(1)}, u32[]{:S(2)}, u32[]{:S(2)}) collective-permute-start(bf16[3,896]{0,1:T(8,128)(2,1)S(1)} %slice.120), channel_id=1, source_target_pairs={{0,4},{4,8},{8,12},{12,16},{16,20},{20,24},{24,28},{28,32},{32,36}... | collective-permute-start | bytes 16136 | tf_op jit(solution)/shard_map/ppermute | solution.py:13
  201.3 11.1 %collective-permute-start.1 = (f32[10,64,128]{2,1,0:T(8,128)S(1)}, f32[10,64,128]{2,1,0:T(8,128)S(1)}, u32[]{:S(2)}, u32[]{:S(2)}) collective-permute-start(f32[10,64,128]{2,1,0:T(8,128)S(1)} %fusion.23), channel_id=1, source_target_pairs={{0,4},{4,8},{8,12},{12,16},{16,20},{20,24},{24,28},{28,32},{32,36}... | collective-permute-start | bytes 983048 | tf_op jit(solution)/shard_map/ppermute | solution.py:13
  205.7 18.5 %collective-permute-start.3 = (f32[10,64,128]{2,1,0:T(8,128)S(1)}, f32[10,64,128]{2,1,0:T(8,128)S(1)}, u32[]{:S(2)}, u32[]{:S(2)}) collective-permute-start(f32[10,64,128]{2,1,0:T(8,128)S(1)} %fusion.23), channel_id=1, source_target_pairs={{0,8},{4,12},{8,16},{12,20},{16,24},{20,28},{24,32},{28,36},{32,40... | collective-permute-start | bytes 983048 | tf_op jit(solution)/shard_map/ppermute | solution.py:13
  208.7 23.2 %collective-permute-start.5 = (f32[10,64,128]{2,1,0:T(8,128)S(1)}, f32[10,64,128]{2,1,0:T(8,128)S(1)}, u32[]{:S(2)}, u32[]{:S(2)}) collective-permute-start(f32[10,64,128]{2,1,0:T(8,128)S(1)} %fusion.23), channel_id=1, source_target_pairs={{0,12},{4,16},{8,20},{12,24},{16,28},{20,32},{24,36},{28,40},{32,4... | collective-permute-start | bytes 983048 | tf_op jit(solution)/shard_map/ppermute | solution.py:13
  211.4 20.7 %copy-start.8 = (f32[10]{0:T(128)S(1)}, f32[10]{0:T(128)}, u32[]{:S(2)}) copy-start(f32[10]{0:T(128)} %param.21) | copy-start | bytes 124
  241.0 1.2 copy-start.1
  241.8 5.9 %copy-start = (bf16[256,640]{0,1:T(8,128)(2,1)S(1)}, bf16[256,640]{0,1:T(8,128)(2,1)}, u32[]{:S(2)}) copy-start(bf16[256,640]{0,1:T(8,128)(2,1)} %get-tuple-element.24) | copy-start | bytes 983044
  243.2 14.1 %all-to-all-start.1 = ((bf16[4,2,1,64,640]{4,3,1,2,0:T(8,128)(2,1)}), bf16[4,2,1,64,640]{4,3,1,2,0:T(8,128)(2,1)S(1)}, u32[]{:S(2)}, u32[]{:S(2)}) async-start(bf16[4,2,1,64,640]{4,3,1,2,0:T(8,128)(2,1)} %pad_maximum_fusion.1), calls=%async_computation.1 | async-start | bytes 1310720 | tf_op jit(solution)/shard_map/all_to_all | solution.py:184
  258.4 0.7 copy-start.3
Sparse Core Ops, SparseCore 0:
  11.7 152.7 all-gather.2
